TPU v7x, 32 devices: a whole 2x2x4 slice. The times are simulated.
32 devices in a mesh: req: 2 (over x), seq: 16 (over z, y, core).
Axes of the slice: x: 2, y: 2, z: 4, core: 2. Of those that a mesh axis runs over, the one named last changes fastest.
Arguments:
- states: bfloat16 [4, 4, 4544], P(None, 'req', 'seq'), may hold values from -6 to 6
- kv_cache: bfloat16 [4, 8192, 128], P('req', 'seq'), may hold values from -48 to 48, as said below
- lengths: int32 [4], replicated, may hold values from 1 to 8188, as said below
- placement: int32 [4], replicated, may hold values from 0 to 3, each once
- norm_gain: bfloat16 [4544], replicated, may hold values from 0.25 to 1.75
- norm_bias: bfloat16 [4544], replicated, may hold values from -1.5 to 1.5
- w_query: bfloat16 [4544, 4544], P('req', 'seq'), may hold values from -0.09375 to 0.09375
- w_keyval: bfloat16 [4544, 128], P('req'), may hold values from -0.09375 to 0.09375
- w_out: bfloat16 [4544, 4544], P('seq', 'req'), may hold values from -0.09375 to 0.09375
- w_up: bfloat16 [4544, 18176], P('req', 'seq'), may hold values from -0.09375 to 0.09375
- w_down: bfloat16 [18176, 4544], P('seq', 'req'), may hold values from -0.046875 to 0.046875
Outputs:
- new_states: bfloat16 [4, 4, 4544], P(None, 'req', 'seq')
- new_cache: bfloat16 [4, 8192, 128], P('req', 'seq')
Inputs may be any that keep to these rules, and one draw needn't show every extreme that they name: Request r's cache holds its first lengths[r] positions; some request has exactly 8188. `kv_cache`: row i is the cache of request placement[i]; positions at or beyond that request's length hold arbitrary values. `placement`: each request is served by exactly one slot.
All inputs are finite; a program needn't handle non-finite values.
Results may differ from a plain program's by a relative error of at most 0.012.
The roundings to bfloat16 on the way count: a program that leaves them out, or rounds other values in their place, can miss the bound.
Values may be sent and summed in bfloat16 or wider, within the bound.
No kernel may reach another device: no remote copies, remote signals or barrier semaphores. Data moves between devices by JAX's collectives and lax.ppermute only.
A program may use at most 192 MiB of HBM per device.

v0:
```python
import jax
import jax.numpy as jnp
from jax import lax
from jax.sharding import PartitionSpec as P

EPSILON = 1e-05
NEGATIVE = -1e30
ALL = ("req", "seq")


def layer_norm(row_block, norm_gain, norm_bias):
    values = row_block.astype(jnp.float32)
    average = jnp.mean(values, axis=-1, keepdims=True)
    centered = values - average
    spread = jnp.mean(centered * centered, axis=-1, keepdims=True)
    scaled = centered * lax.rsqrt(spread + EPSILON)
    return (scaled * norm_gain.astype(jnp.float32) + norm_bias.astype(jnp.float32)).astype(
        jnp.bfloat16
    )


def rotate(vectors, positions):
    head_width = vectors.shape[-1]
    half_width = head_width // 2
    frequency = 10000.0 ** (-(jnp.arange(half_width, dtype=jnp.float32) * 2.0) / head_width)
    angles = positions.astype(jnp.float32)[:, None] * frequency[None, :]
    cosine = jnp.concatenate([jnp.cos(angles), jnp.cos(angles)], axis=-1)[:, None, :]
    sine_wave = jnp.concatenate([jnp.sin(angles), jnp.sin(angles)], axis=-1)[:, None, :]
    turned = jnp.concatenate([-vectors[..., half_width:], vectors[..., :half_width]], axis=-1)
    return vectors * cosine + turned * sine_wave


def shards(
    states,
    kv_cache,
    lengths,
    placement,
    norm_gain,
    norm_bias,
    w_query,
    w_keyval,
    w_out,
    w_up,
    w_down,
):
    steps = states.shape[0]
    group_rows = kv_cache.shape[0]
    seg_length = kv_cache.shape[1]
    head_width = kv_cache.shape[2] // 2
    model_width = norm_gain.shape[0]
    head_count = model_width // head_width
    slice_width = states.shape[2]
    part_width = w_query.shape[0]
    total = placement.shape[0]
    req_size = total // group_rows
    seq_size = model_width // slice_width
    rows = steps * total
    group_index = lax.axis_index("req")
    shard_index = lax.axis_index("seq")
    own_requests = lax.dynamic_slice_in_dim(placement, group_index * group_rows, group_rows, 0)
    slot_lengths = jnp.take(lengths, own_requests)
    step_offsets = jnp.arange(steps, dtype=jnp.int32)
    positions = slot_lengths[None, :] + step_offsets[:, None]
    every = lax.all_gather(states, ALL, axis=0, tiled=False)
    every = every.reshape(req_size, seq_size, steps, group_rows, slice_width)
    every = every.transpose(2, 0, 3, 1, 4).reshape(steps, total, model_width)
    current_all = jnp.take(every, placement, axis=1)
    normed = layer_norm(current_all.reshape(rows, model_width), norm_gain, norm_bias)
    normed_part = lax.dynamic_slice_in_dim(normed, group_index * part_width, part_width, 1)
    part_query = jnp.dot(normed_part, w_query, preferred_element_type=jnp.float32)
    part_keyval = jnp.dot(normed_part, w_keyval, preferred_element_type=jnp.float32)
    part_up = jnp.dot(normed_part, w_up, preferred_element_type=jnp.float32)
    first = lax.psum(jnp.concatenate([part_query, part_keyval, part_up], axis=1), "req")
    query_raw = first[:, :slice_width].astype(jnp.bfloat16).reshape(steps, total, slice_width)
    keyval = first[:, slice_width : slice_width + 2 * head_width].reshape(
        steps, total, 2 * head_width
    )
    up_part = first[:, slice_width + 2 * head_width :]
    own_query = lax.dynamic_slice_in_dim(query_raw, group_index * group_rows, group_rows, 1)
    query_all = lax.all_gather(own_query, "seq", axis=2, tiled=True)
    flat_positions = positions.reshape(-1)
    query_rows = rotate(
        query_all.astype(jnp.float32).reshape(steps * group_rows, head_count, head_width),
        flat_positions,
    ).astype(jnp.bfloat16)
    own_keyval = lax.dynamic_slice_in_dim(keyval, group_index * group_rows, group_rows, 1)
    own_keyval = own_keyval.reshape(steps * group_rows, 2 * head_width)
    new_key = rotate(own_keyval[:, None, :head_width], flat_positions)[:, 0, :]
    new_entry = jnp.concatenate([new_key, own_keyval[:, head_width:]], axis=-1).astype(jnp.bfloat16)
    new_entry = new_entry.reshape(steps, group_rows, 2 * head_width)
    local_slots = jnp.arange(seg_length, dtype=jnp.int32)
    global_positions = shard_index * seg_length + local_slots
    cache_now = kv_cache
    for step_index in range(steps):
        write_mask = global_positions[None, :] == positions[step_index][:, None]
        cache_now = jnp.where(write_mask[:, :, None], new_entry[step_index][:, None, :], cache_now)
    key_rows = cache_now[:, :, :head_width]
    value_rows = cache_now[:, :, head_width:]
    query_heads = (
        query_rows.reshape(steps, group_rows, head_count, head_width)
        .transpose(1, 0, 2, 3)
        .reshape(group_rows, steps * head_count, head_width)
    )
    scores = jnp.einsum(
        "gqd,gsd->gqs", query_heads, key_rows, preferred_element_type=jnp.float32
    ) * head_width ** (-0.5)
    valid = global_positions[None, None, :] <= positions.T[:, :, None]
    valid = jnp.broadcast_to(
        valid[:, :, None, :], (group_rows, steps, head_count, seg_length)
    ).reshape(group_rows, steps * head_count, seg_length)
    local_peak = jnp.max(jnp.where(valid, scores, NEGATIVE), axis=-1)
    weights = jnp.where(valid, jnp.exp(scores - local_peak[:, :, None]), 0.0)
    local_total = jnp.sum(weights, axis=-1)
    local_weighted = jnp.einsum(
        "gqs,gsd->gqd", weights, value_rows, preferred_element_type=jnp.float32
    )
    peak_buffer = jnp.full((total, steps * head_count), NEGATIVE, jnp.float32)
    peak_buffer = lax.dynamic_update_slice_in_dim(
        peak_buffer, local_peak, group_index * group_rows, 0
    )
    peak = lax.pmax(peak_buffer, ALL)
    own_peak = lax.dynamic_slice_in_dim(peak, group_index * group_rows, group_rows, 0)
    scale = jnp.exp(local_peak - own_peak)
    packed = jnp.concatenate(
        [local_weighted * scale[:, :, None], (local_total * scale)[:, :, None]], axis=-1
    )
    packed_buffer = jnp.zeros((total, steps * head_count, head_width + 1), jnp.float32)
    packed_buffer = lax.dynamic_update_slice_in_dim(
        packed_buffer, packed, group_index * group_rows, 0
    )
    summed = lax.psum(packed_buffer, ALL)
    mixed = summed[:, :, :head_width] / summed[:, :, head_width:]
    mixed = (
        mixed.reshape(total, steps, model_width)
        .transpose(1, 0, 2)
        .reshape(rows, model_width)
        .astype(jnp.bfloat16)
    )
    mixed_part = lax.dynamic_slice_in_dim(mixed, shard_index * slice_width, slice_width, 1)
    hidden = jax.nn.gelu(up_part, approximate=False).astype(jnp.bfloat16)
    partial_sum = jnp.dot(mixed_part, w_out, preferred_element_type=jnp.float32) + jnp.dot(
        hidden, w_down, preferred_element_type=jnp.float32
    )
    out_buffer = jnp.zeros((rows, model_width), jnp.float32)
    out_buffer = lax.dynamic_update_slice_in_dim(
        out_buffer, partial_sum, group_index * part_width, 1
    )
    branch = lax.psum(out_buffer, ALL).reshape(steps, total, model_width)
    inverse = jnp.zeros((total,), jnp.int32).at[placement].set(jnp.arange(total, dtype=jnp.int32))
    own_inverse = lax.dynamic_slice_in_dim(inverse, group_index * group_rows, group_rows, 0)
    own_branch = jnp.take(branch, own_inverse, axis=1)
    own_branch = lax.dynamic_slice_in_dim(own_branch, shard_index * slice_width, slice_width, 2)
    new_states = (states.astype(jnp.float32) + own_branch).astype(jnp.bfloat16)
    return (new_states, cache_now)


def solution(mesh):
    in_specs = (
        P(None, "req", "seq"),
        P("req", "seq", None),
        P(),
        P(),
        P(),
        P(),
        P("req", "seq"),
        P("req", None),
        P("seq", "req"),
        P("req", "seq"),
        P("seq", "req"),
    )
    out_specs = (P(None, "req", "seq"), P("req", "seq", None))
    return jax.shard_map(shards, mesh=mesh, in_specs=in_specs, out_specs=out_specs, check_vma=False)
```

profile of v0, /device:TPU:8, one launch (start us, length us, event | category | flops | bytes accessed | tf_op | source)
XLA Modules:
  0.0 437.4 jit_solution(13402356280962080718)
XLA Ops:
  7.2 0.8 compare_select_fusion.2
  8.0 0.7 compare_and_fusion
  8.6 0.8 dynamic-slice.1
  9.4 0.8 dynamic-slice.2
  10.2 38.8 %all-gather = bf16[128,2,284]{2,1,0:T(2,128)(2,1)S(1)} all-gather(bf16[4,2,284]{2,1,0:T(2,128)(2,1)} %param.11), channel_id=2, replica_groups=mesh['req'=2,'seq'=16] {'req','seq'}, dimensions={0}, use_global_device_ids=true | all-gather | bytes 149952 | tf_op jit(solution)/shard_map/all_gather | solution.py:64
  49.0 0.3 reshape.348
  49.4 0.7 gather_fusion.1
  50.1 0.3 convert_reduce_fusion
  50.4 0.3 fusion.5
  51.3 3.5 fusion.96
  54.8 0.3 fusion.94
  55.1 0.4 fusion.95
  55.5 0.8 concatenate.40
  56.5 0.6 gather_fusion
  57.7 0.1 copy.81
  58.0 0.2 reshape.346
  58.3 19.3 %all-reduce.4.cloned.1.call-done = f32[16,1548]{1,0:T(8,128)} async-done(((f32[16,1548]{1,0:T(8,128)}), f32[16,1548]{1,0:T(8,128)}) %all-reduce.4.cloned.1.call-update) | async-done | bytes 99088 | tf_op jit(solution)/shard_map/psum | solution.py:73
  77.6 0.8 slice.99
  78.4 0.7 slice.124
  79.2 0.2 copy.88
  79.4 32.2 %all_gather.11 = bf16[4,2,4544]{0,1,2:T(2,128)(2,1)} all-gather(bf16[4,2,284]{0,1,2:T(2,128)(2,1)S(1)} %copy.88), channel_id=1, replica_groups=mesh['req'=2,'seq'=16] {'seq'}, dimensions={2}, use_global_device_ids=true | all-gather | bytes 77248 | tf_op jit(solution)/shard_map/all_gather | solution.py:80
  111.6 5.2 %copy.73 = bf16[4,2,4544]{2,0,1:T(4,128)(2,1)S(1)} copy(bf16[4,2,4544]{0,1,2:T(2,128)(2,1)} %all_gather.11) | data formatting | bytes 145408 | tf_op jit(solution)/shard_map/all_gather | solution.py:80
  116.8 0.2 reshape.351
  117.1 0.2 reshape.350
  117.9 0.2 copy.78
  118.1 0.2 fusion.8
  118.2 0.2 copy.80
  118.5 0.2 select_select_fusion
  118.8 0.5 select_reduce_fusion
  119.3 41.3 %pmax.7 = f32[4,284]{1,0:T(4,128)S(1)} all-reduce(f32[4,284]{1,0:T(4,128)S(1)} %constant_dynamic-update-slice_fusion.1), channel_id=1, replica_groups=mesh['req'=2,'seq'=16] {'req','seq'}, use_global_device_ids=true, to_apply=%region_5.6 | all-reduce | flops 1136 | bytes 9088 | tf_op jit(solution)/shard_map/pmax | solution.py:121
  160.6 0.4 fusion
  161.0 0.4 convolution_multiply_fusion.1
  161.5 0.2 copy.82
  161.7 0.8 copy-done.2
  162.6 0.6 scatter_custom_fusion
  163.2 129.3 %all-reduce.6.cloned.1.call-done = f32[4,284,65]{2,1,0:T(8,128)} async-done(((f32[4,284,65]{2,1,0:T(8,128)}), f32[4,284,65]{2,1,0:T(8,128)}) %all-reduce.6.cloned.1.call-update) | async-done | bytes 295376 | tf_op jit(solution)/shard_map/psum | solution.py:131
  292.5 1.5 slice_reduce_fusion
  294.0 1.3 fusion.1
  295.3 0.2 convert_element_type.69
  295.6 0.4 fusion.55
  296.0 0.2 copy-done.6
  296.2 3.4 convolution_add_fusion
  299.7 1.3 dynamic_update_slice.11
  301.1 0.8 copy.84
  302.0 0.8 copy.86
  302.9 125.7 %all-reduce.8.cloned.1.call-done = f32[4,4,4544]{2,0,1:T(4,128)} async-done(((f32[4,4,4544]{2,0,1:T(4,128)}), f32[4,4,4544]{2,0,1:T(4,128)}) %all-reduce.8.cloned.1.call-update) | async-done | bytes 290832 | tf_op jit(solution)/shard_map/psum | solution.py:148
  428.5 1.6 gather_fusion.2
  430.2 0.6 copy.85
  (81 shorter events, 3.2 us)
Async XLA Ops:
  7.2 288.4 %copy-start = (bf16[284,2272]{1,0:T(8,128)(2,1)S(1)}, bf16[284,2272]{1,0:T(8,128)(2,1)}, u32[]{:S(2)}) copy-start(bf16[284,2272]{1,0:T(8,128)(2,1)} %param.19) | copy-start | bytes 3871492
  7.2 70.4 %all-reduce.4.cloned.1.call-start = ((), (), s32[]{:S(2)}) async-start(), calls=%async_computation | async-start | bytes 212992 | tf_op jit(solution)/shard_map/psum | solution.py:73
  51.3 3.5 copy-start.4
  51.3 3.8 copy-start.3
  54.8 1.6 copy-start.8
  54.8 1.7 copy-start.1
  55.1 2.6 copy-start.5
  56.3 236.2 %all-reduce.6.cloned.1.call-start = ((), (), s32[]{:S(2)}) async-start(), calls=%async_computation.1 | async-start | bytes 1179648 | tf_op jit(solution)/shard_map/psum | solution.py:131
  161.7 0.8 copy-start.2
  162.6 266.0 %all-reduce.8.cloned.1.call-start = ((), (), s32[]{:S(2)}) async-start(), calls=%async_computation.2 | async-start | bytes 589824 | tf_op jit(solution)/shard_map/psum | solution.py:148
  295.3 0.9 copy-start.6
  301.0 129.2 %copy-start.7 = (bf16[4,2,284]{2,1,0:T(2,128)(2,1)S(1)}, bf16[4,2,284]{2,1,0:T(2,128)(2,1)}, u32[]{:S(2)}) copy-start(bf16[4,2,284]{2,1,0:T(2,128)(2,1)} %param.11) | copy-start | bytes 13636
Sparse Core Ops, SparseCore 0:
  56.4 21.1 all-reduce.3
  162.7 129.7 all-reduce.5
  302.1 126.4 all-reduce.7
where the time goes:
time: 438 us; the launch traced here: 437 us
  waiting for transfers between devices  274 us (63%)
  blocking collectives  112 us (26%)
  local copies, waits for them, and re-layouts  22.3 us (5%)
  between operations  14.2 us (3%)
  matrix products  8.89 us (2%)
  other arithmetic  5.32 us (1%)
    psum x1, waiting for transfers between devices, shards(): summed = lax.psum(packed_buffer, ALL)  129 us
    psum x1, waiting for transfers between devices, shards(): branch = lax.psum(out_buffer, ALL).reshape(steps, total, model_width)  126 us
    pmax x1, blocking collectives, shards(): peak = lax.pmax(peak_buffer, ALL)  41.3 us
    all_gather x1, blocking collectives, shards(): every = lax.all_gather(states, ALL, axis=0, tiled=False)  38.8 us
    all_gather x1, blocking collectives, shards(): query_all = lax.all_gather(own_query, 'seq', axis=2, tiled=True)  32.2 us
    psum x1, waiting for transfers between devices, shards(): lax.psum(jnp.concatenate([part_query, part_keyval, part_up], axis=1), 'req')  19.3 us
  transfers between devices with their start and end apart: 3, of which 3 were waited for; matrix products, arithmetic and copies ran while one was open for 1% of the time, Pallas kernels for 0%

commit v1 on v0

--- a/solution.py
+++ b/solution.py
@@ -6,6 +6,19 @@
 EPSILON = 1e-05
 NEGATIVE = -1e30
 ALL = ("req", "seq")
+
+
+def ring_gather(shard, axis, dim):
+    ways = lax.axis_size(axis)
+    up = [(d, (d + 1) % ways) for d in range(ways)]
+    down = [(d, (d - 1) % ways) for d in range(ways)]
+    earlier, later = ([shard], [shard])
+    for _ in range(ways // 2):
+        earlier.append(lax.ppermute(earlier[-1], axis, up))
+    for _ in range((ways - 1) // 2):
+        later.append(lax.ppermute(later[-1], axis, down))
+    line = jnp.concatenate([*earlier[::-1], *later[1:]], axis=dim)
+    return jnp.roll(line, (lax.axis_index(axis) - ways // 2) * shard.shape[dim], axis=dim)
 
 
 def layer_norm(row_block, norm_gain, norm_bias):
@@ -77,7 +90,7 @@
     )
     up_part = first[:, slice_width + 2 * head_width :]
     own_query = lax.dynamic_slice_in_dim(query_raw, group_index * group_rows, group_rows, 1)
-    query_all = lax.all_gather(own_query, "seq", axis=2, tiled=True)
+    query_all = ring_gather(own_query, "seq", 2)
     flat_positions = positions.reshape(-1)
     query_rows = rotate(
         query_all.astype(jnp.float32).reshape(steps * group_rows, head_count, head_width),

time: 438 us -> 441 us (level)
  blocking collectives: 112 us -> 91.6 us
  starting transfers between devices: 0.12 us -> 18.5 us
  waiting for transfers between devices: 274 us -> 285 us
  local copies, waits for them, and re-layouts: 22.3 us -> 16.8 us
    all_gather x1 -> x0, blocking collectives: 32.2 us -> none  [shards(): query_all = lax.all_gather(own_query, 'seq', axis=2, tiled=True)]
    ppermute x0 -> x15, starting transfers between devices: none -> 18.4 us  [the longest x7 18.3 us: ring_gather(): later.append(lax.ppermute(later[-1], axis, down))]
    ppermute x0 -> x15, waiting for transfers between devices: none -> 12.1 us  [the longest x8 8.3 us: ring_gather(): earlier.append(lax.ppermute(earlier[-1], axis, up))]
    pmax x1, blocking collectives: 41.3 us -> 52.7 us  [shards(): peak = lax.pmax(peak_buffer, ALL)]
    all_gather x1 -> x0, local copies, waits for them, and re-layouts: 5.18 us -> none  [shards(): query_all = lax.all_gather(own_query, 'seq', axis=2, tiled=True)]
  transfers between devices with their start and end apart: 3 -> 18, of which waited for: 3 -> 18; matrix products, arithmetic and copies ran while one was open for 1% -> 1% of each run, Pallas kernels for 0% -> 0%
where the time goes in v1:
time: 441 us; the launch traced here: 440 us
  waiting for transfers between devices  285 us (65%)
  blocking collectives  91.6 us (21%)
  starting transfers between devices  18.5 us (4%)
  local copies, waits for them, and re-layouts  16.8 us (4%)
  between operations  14.2 us (3%)
  matrix products  8.91 us (2%)
  other arithmetic  5.47 us (1%)
    psum x1, waiting for transfers between devices, shards(): summed = lax.psum(packed_buffer, ALL)  127 us
    psum x1, waiting for transfers between devices, shards(): branch = lax.psum(out_buffer, ALL).reshape(steps, total, model_width)  126 us
    pmax x1, blocking collectives, shards(): peak = lax.pmax(peak_buffer, ALL)  52.7 us
    all_gather x1, blocking collectives, shards(): every = lax.all_gather(states, ALL, axis=0, tiled=False)  38.8 us
    psum x1, waiting for transfers between devices, shards(): lax.psum(jnp.concatenate([part_query, part_keyval, part_up], axis=1), 'req')  19.8 us
    ppermute x7, starting transfers between devices, ring_gather(): later.append(lax.ppermute(later[-1], axis, down))  18.3 us
  transfers between devices with their start and end apart: 18, of which 18 were waited for; matrix products, arithmetic and copies ran while one was open for 1% of the time, Pallas kernels for 0%

profile of v1, /device:TPU:8, one launch (start us, length us, event | category | flops | bytes accessed | tf_op | source)
XLA Modules:
  0.0 440.2 jit_solution(4003512747628434265)
XLA Ops:
  7.2 0.8 compare_select_fusion.2
  8.0 0.7 compare_and_fusion
  8.6 0.8 dynamic-slice.1
  9.4 0.8 dynamic-slice.2
  10.2 38.8 %all-gather = bf16[128,2,284]{2,1,0:T(2,128)(2,1)S(1)} all-gather(bf16[4,2,284]{2,1,0:T(2,128)(2,1)} %param.11), channel_id=2, replica_groups=mesh['req'=2,'seq'=16] {'req','seq'}, dimensions={0}, use_global_device_ids=true | all-gather | bytes 149952 | tf_op jit(solution)/shard_map/all_gather | solution.py:77
  49.4 0.7 gather_fusion.1
  51.3 3.5 fusion.96
  55.1 0.4 fusion.95
  55.5 0.8 concatenate.46
  56.5 0.6 gather_fusion
  57.8 19.8 %all-reduce.4.cloned.1.call-done = f32[16,1548]{1,0:T(8,128)} async-done(((f32[16,1548]{1,0:T(8,128)}), f32[16,1548]{1,0:T(8,128)}) %all-reduce.4.cloned.1.call-update) | async-done | bytes 99088 | tf_op jit(solution)/shard_map/psum | solution.py:86
  77.6 0.8 slice.124
  79.0 2.7 collective-permute-start.8
  81.8 0.6 collective-permute-done
  82.5 0.6 collective-permute-done.8
  83.1 2.6 collective-permute-start.9
  85.7 0.7 collective-permute-done.1
  86.4 0.6 collective-permute-done.9
  87.0 2.6 collective-permute-start.10
  89.6 0.7 collective-permute-done.2
  90.4 0.5 collective-permute-done.10
  91.0 2.6 collective-permute-start.11
  93.6 0.7 collective-permute-done.3
  94.5 0.5 collective-permute-done.11
  94.9 2.6 collective-permute-start.12
  97.5 0.7 collective-permute-done.4
  98.3 0.5 collective-permute-done.12
  98.9 2.6 collective-permute-start.13
  101.5 0.7 collective-permute-done.5
  102.2 0.6 collective-permute-done.13
  102.8 2.6 collective-permute-start.14
  105.5 0.7 collective-permute-done.6
  106.8 3.3 collective-permute-done.7
  110.1 0.8 concatenate.47
  112.5 0.5 select_reduce_fusion
  113.1 52.7 %pmax.7 = f32[4,284]{1,0:T(4,128)S(1)} all-reduce(f32[4,284]{1,0:T(4,128)S(1)} %constant_dynamic-update-slice_fusion.1), channel_id=1, replica_groups=mesh['req'=2,'seq'=16] {'req','seq'}, use_global_device_ids=true, to_apply=%region_5.6 | all-reduce | flops 1136 | bytes 9088 | tf_op jit(solution)/shard_map/pmax | solution.py:134
  167.0 0.8 copy-done.2
  167.9 0.6 scatter_custom_fusion
  168.4 127.1 %all-reduce.6.cloned.1.call-done = f32[4,284,65]{2,1,0:T(8,128)} async-done(((f32[4,284,65]{2,1,0:T(8,128)}), f32[4,284,65]{2,1,0:T(8,128)}) %all-reduce.6.cloned.1.call-update) | async-done | bytes 295376 | tf_op jit(solution)/shard_map/psum | solution.py:144
  295.5 1.5 slice_reduce_fusion
  297.0 1.3 fusion.1
  299.0 3.4 convolution_add_fusion
  302.5 1.3 dynamic_update_slice.11
  303.9 0.8 copy.77
  304.8 0.8 copy.79
  305.7 125.7 %all-reduce.8.cloned.1.call-done = f32[4,4,4544]{2,0,1:T(4,128)} async-done(((f32[4,4,4544]{2,0,1:T(4,128)}), f32[4,4,4544]{2,0,1:T(4,128)}) %all-reduce.8.cloned.1.call-update) | async-done | bytes 290832 | tf_op jit(solution)/shard_map/psum | solution.py:161
  431.3 1.6 gather_fusion.2
  433.0 0.6 copy.78
  (109 shorter events, 7.9 us)
Async XLA Ops:
  7.2 291.5 %copy-start = (bf16[284,2272]{1,0:T(8,128)(2,1)S(1)}, bf16[284,2272]{1,0:T(8,128)(2,1)}, u32[]{:S(2)}) copy-start(bf16[284,2272]{1,0:T(8,128)(2,1)} %param.19) | copy-start | bytes 3871492
  7.2 70.4 %all-reduce.4.cloned.1.call-start = ((), (), s32[]{:S(2)}) async-start(), calls=%async_computation | async-start | bytes 212992 | tf_op jit(solution)/shard_map/psum | solution.py:86
  51.3 3.5 copy-start.4
  51.3 3.8 copy-start.3
  54.8 1.6 copy-start.8
  54.8 1.7 copy-start.1
  55.1 23.5 %copy-start.5 = (bf16[2,512,128]{2,1,0:T(8,128)(2,1)S(1)}, bf16[2,512,128]{2,1,0:T(8,128)(2,1)}, u32[]{:S(2)}) copy-start(bf16[2,512,128]{2,1,0:T(8,128)(2,1)} %param.12) | copy-start | bytes 786436
  56.3 239.2 %all-reduce.6.cloned.1.call-start = ((), (), s32[]{:S(2)}) async-start(), calls=%async_computation.1 | async-start | bytes 1179648 | tf_op jit(solution)/shard_map/psum | solution.py:144
  77.6 4.1 copy-start.6
  78.4 4.0 collective-permute-start
  79.0 4.0 collective-permute-start.8
  82.4 4.0 collective-permute-start.1
  83.1 4.0 collective-permute-start.9
  86.4 4.0 collective-permute-start.2
  87.0 4.0 collective-permute-start.10
  90.4 4.0 collective-permute-start.3
  91.0 4.0 collective-permute-start.11
  94.3 4.0 collective-permute-start.4
  94.9 4.0 collective-permute-start.12
  98.3 4.0 collective-permute-start.5
  98.9 4.0 collective-permute-start.13
  102.2 4.0 collective-permute-start.6
  102.8 4.0 collective-permute-start.14
  106.2 4.0 collective-permute-start.7
  167.0 0.8 copy-start.2
  167.8 263.5 %all-reduce.8.cloned.1.call-start = ((), (), s32[]{:S(2)}) async-start(), calls=%async_computation.2 | async-start | bytes 589824 | tf_op jit(solution)/shard_map/psum | solution.py:161
  303.8 129.2 %copy-start.7 = (bf16[4,2,284]{2,1,0:T(2,128)(2,1)S(1)}, bf16[4,2,284]{2,1,0:T(2,128)(2,1)}, u32[]{:S(2)}) copy-start(bf16[4,2,284]{2,1,0:T(2,128)(2,1)} %param.11) | copy-start | bytes 13636
Sparse Core Ops, SparseCore 0:
  56.4 21.1 all-reduce.3
  167.9 127.5 all-reduce.5
  304.9 126.4 all-reduce.7
